TPU v7x, 512 devices: a whole 4x4x16 slice. The times are simulated.
512 devices in a mesh: clip: 16 (over y, z_hi), seq: 32 (over x, z_lo, core).
Axes of the slice: x: 4, y: 4, z: 16 (z_hi: 4, z_lo: 4; z = z_hi * 4 + z_lo), core: 2. Of those that a mesh axis runs over, the one named last changes fastest.
Arguments:
- frames_in: bfloat16 [512, 256, 1152], P(('clip', 'seq')), parts along dimension 0, may hold values from -6 to 6
- modulation: float32 [48, 1152], P('clip'), parts along dimension 0, may hold values from -3 to 3
- self_proj: bfloat16 [1152, 1728], P(None, 'seq'), may hold values from -0.1875 to 0.1875
- self_out: bfloat16 [576, 1152], P(None, 'seq'), may hold values from -0.25 to 0.25
- cross_query: bfloat16 [1152, 576], P(None, 'seq'), may hold values from -0.1875 to 0.1875
- cross_keyval: bfloat16 [1152, 1152], P(None, 'seq'), may hold values from -0.1875 to 0.1875
- cross_out: bfloat16 [576, 1152], P(None, 'seq'), may hold values from -0.25 to 0.25
- text_bank: bfloat16 [32, 256, 1152], P('seq'), may hold values from -6 to 6
- prompt_pick: int32 [16], P('clip'), parts along dimension 0, may hold values from 0 to 31
- text_lengths: int32 [32], replicated, may hold values from 32 to 256
Outputs:
- frames_out: bfloat16 [512, 256, 1152], P(('clip', 'seq')), parts along dimension 0
There are 16 independent parts, one for each index of `clip`. A program takes and returns all parts, laid end to end along the dimension named above; an argument that names none is the same for every part. Nothing has to cross between parts.
All inputs are finite; a program needn't handle non-finite values.
Results may differ from a plain program's by a relative error of at most 0.006.
Values may be sent and summed in bfloat16 or wider, within the bound.
No kernel may reach another device: no remote copies, remote signals or barrier semaphores. Data moves between devices by JAX's collectives and lax.ppermute only.
A program may use at most 64 MiB of HBM per device.

v0:
```python
import math
import jax
import jax.numpy as jnp
from jax import lax
from jax.sharding import PartitionSpec as P

HEAD_DIM = 72
EPS = 1e-06


def spread_2(block, axis, owner):
    block = jnp.where(lax.axis_index(axis) == owner, block, jnp.zeros_like(block))
    return lax.psum(block, axis)


def layer_norm(values):
    mean = jnp.mean(values, axis=-1, keepdims=True)
    centred = values - mean
    spread = jnp.mean(centred * centred, axis=-1, keepdims=True)
    return centred * lax.rsqrt(spread + EPS)


def head_norm(values, heads):
    shaped = values.reshape(values.shape[:-1] + (heads, values.shape[-1] // heads))
    power = jnp.mean(shaped * shaped, axis=-1, keepdims=True)
    return shaped * lax.rsqrt(power + EPS)


def temporal_attention(qkv, heads, attn, scale_q):
    frames, patches = (qkv.shape[0], qkv.shape[1])
    query = (head_norm(qkv[..., :attn].astype(jnp.float32), heads) * scale_q).astype(jnp.bfloat16)
    key = head_norm(qkv[..., attn : 2 * attn].astype(jnp.float32), heads).astype(jnp.bfloat16)
    value = qkv[..., 2 * attn :].reshape(frames, patches, heads, attn // heads)
    scores = jnp.einsum("fphd,gphd->phfg", query, key, preferred_element_type=jnp.float32)
    weights = jnp.exp(scores)
    total = jnp.sum(weights, axis=-1)
    probs = weights.astype(jnp.bfloat16)
    mixed = jnp.einsum("phfg,gphd->fphd", probs, value, preferred_element_type=jnp.float32)
    attended = mixed / jnp.transpose(total, (2, 0, 1))[..., None]
    return attended.astype(jnp.bfloat16).reshape(frames, patches, attn)


def per_device(
    frames_in,
    modulation,
    self_proj,
    self_out,
    cross_query,
    cross_keyval,
    cross_out,
    text_bank,
    prompt_pick,
    text_lengths,
):
    count = lax.axis_size("seq")
    frame_rows, pixels, width = frames_in.shape
    attn = self_out.shape[0]
    heads = attn // HEAD_DIM
    scale_q = 1.0 / math.sqrt(HEAD_DIM)
    pix_dev = pixels // count
    frames = frame_rows * count
    tokens = frames_in.astype(jnp.float32)
    normed = (layer_norm(tokens) * (1.0 + modulation[1]) + modulation[0]).astype(jnp.bfloat16)
    switched = lax.all_to_all(normed, "seq", split_axis=1, concat_axis=0, tiled=True)
    flat_pix = switched.reshape(-1, width)
    qkv = jnp.dot(
        flat_pix,
        lax.all_gather(self_proj, "seq", axis=1, tiled=True),
        preferred_element_type=jnp.float32,
    ).astype(jnp.bfloat16)
    qkv = qkv.reshape(frames, pix_dev, 3 * attn)
    out_self, query_weight, out_cross = (
        lax.all_gather(self_out, "seq", axis=1, tiled=True),
        lax.all_gather(cross_query, "seq", axis=1, tiled=True),
        lax.all_gather(cross_out, "seq", axis=1, tiled=True),
    )
    attended = temporal_attention(qkv, heads, attn, scale_q)
    returned = lax.all_to_all(attended, "seq", split_axis=0, concat_axis=1, tiled=True)
    self_term = jnp.dot(returned.reshape(-1, attn), out_self, preferred_element_type=jnp.float32)
    after_self = (tokens.reshape(-1, width) + modulation[2] * self_term).astype(jnp.bfloat16)
    pick = prompt_pick[0]
    memory = spread_2(text_bank[0], "seq", pick)
    own_columns = jnp.dot(memory, cross_keyval, preferred_element_type=jnp.float32).astype(
        jnp.bfloat16
    )
    keyval = lax.all_gather(own_columns, "seq", axis=1, tiled=True)
    text_len = keyval.shape[0]
    text_key = head_norm(keyval[:, :attn].astype(jnp.float32), heads).astype(jnp.bfloat16)
    text_value = keyval[:, attn:].reshape(text_len, heads, HEAD_DIM)
    slots = jnp.arange(text_lengths.shape[0], dtype=jnp.int32)
    length = jnp.sum(jnp.where(slots == pick, text_lengths, 0))
    live = jnp.arange(text_len, dtype=jnp.int32) < length
    text_query = jnp.dot(after_self, query_weight, preferred_element_type=jnp.float32)
    text_query = (head_norm(text_query, heads) * scale_q).astype(jnp.bfloat16)
    cross_scores = jnp.einsum(
        "thd,lhd->thl", text_query, text_key, preferred_element_type=jnp.float32
    )
    cross_weights = jnp.where(live, jnp.exp(cross_scores), 0.0)
    cross_total = jnp.sum(cross_weights, axis=-1)
    cross_probs = cross_weights.astype(jnp.bfloat16)
    cross_mix = jnp.einsum(
        "thl,lhd->thd", cross_probs, text_value, preferred_element_type=jnp.float32
    )
    crossed = (cross_mix / cross_total[..., None]).astype(jnp.bfloat16).reshape(-1, attn)
    cross_term = jnp.dot(crossed, out_cross, preferred_element_type=jnp.float32)
    frames_out = (after_self.astype(jnp.float32) + cross_term).astype(jnp.bfloat16)
    return frames_out.reshape(frame_rows, pixels, width)


def solution(mesh):
    placed = (
        P(("clip", "seq"), None, None),
        P("clip", None),
        P(None, "seq"),
        P(None, "seq"),
        P(None, "seq"),
        P(None, "seq"),
        P(None, "seq"),
        P("seq", None, None),
        P("clip"),
        P(),
    )
    return jax.shard_map(
        per_device,
        mesh=mesh,
        in_specs=placed,
        out_specs=P(("clip", "seq"), None, None),
        check_vma=False,
    )
```

profile of v0, /device:TPU:1, one launch (start us, length us, event | category | flops | bytes accessed | tf_op | source)
XLA Modules:
  0.0 582.2 jit_solution(11461628995922027875)
XLA Ops:
  6.5 0.0 copy-start
  6.5 0.7 all-gather.10.cloned.1.call-update
  7.3 0.0 all-reduce.2.cloned.1.call-start
  8.0 0.9 select_bitcast_fusion
  8.8 0.0 all-reduce.2.cloned.1.call-update
  8.9 0.0 all-gather.12.cloned.1.call-start
  8.9 0.7 all-gather.12.cloned.1.call-update
  9.6 0.0 all-gather.14.cloned.1.call-start
  9.6 0.5 all-gather.14.cloned.1.call-update
  10.2 0.0 copy-done.6
  10.2 0.0 copy-done.1
  10.2 0.2 convert_reduce_fusion
  10.4 0.3 fusion.10
  10.7 0.3 fusion.13
  11.0 0.9 copy.54
  12.0 0.6 broadcast.113
  12.5 4.3 reduce.8
  16.9 0.0 copy-start.7
  16.9 1.0 reshape.164
  17.9 10.4 %all-to-all-start = ((bf16[32,2,4608]{2,1,0:T(2,128)(2,1)}), bf16[32,2,4608]{2,1,0:T(2,128)(2,1)S(1)}, u32[]{:S(2)}, u32[]{:S(2)}) async-start(bf16[32,2,4608]{2,1,0:T(2,128)(2,1)} %reshape.164), calls=%async_computation | async-start | bytes 1179648 | tf_op jit(solution)/shard_map/all_to_all | solution.py:64
  28.4 0.2 all-gather.16.cloned.1.call-start
  28.6 0.4 all-gather.16.cloned.1.call-update
  29.0 0.6 fusion.31
  29.6 20.2 %all-to-all-done = bf16[32,2,4608]{2,1,0:T(2,128)(2,1)S(1)} async-done(((bf16[32,2,4608]{2,1,0:T(2,128)(2,1)}), bf16[32,2,4608]{2,1,0:T(2,128)(2,1)S(1)}, u32[]{:S(2)}, u32[]{:S(2)}) %all-to-all-start) | async-done | bytes 589856 | tf_op jit(solution)/shard_map/all_to_all | solution.py:64
  49.7 0.5 reshape.165
  50.2 37.1 %all-gather.10.cloned.1.call-done = bf16[32,54,1152]{2,1,0:T(8,128)(2,1)} async-done(((bf16[1,54,1152]{2,1,0:T(8,128)(2,1)}), bf16[32,54,1152]{2,1,0:T(8,128)(2,1)}) %all-gather.10.cloned.1.call-update) | async-done | bytes 3981328 | tf_op jit(solution)/shard_map/all_gather | solution.py:68
  87.3 5.0 reshape.150
  92.3 3.5 convolution_convert_fusion
  95.8 0.6 copy.29
  96.5 0.9 slice_convert_fusion.1
  97.3 0.5 reshape.146
  97.8 1.0 multiply_reduce_fusion
  98.8 0.5 reshape.144
  99.3 1.6 reshape.130
  100.9 0.3 multiply_reduce_fusion.1
  101.3 0.7 multiply_convert_fusion
  102.0 0.9 fusion.35
  102.9 0.7 fusion.7
  103.6 0.2 copy.34
  103.9 1.1 reshape.135
  104.9 6.6 %all-to-all-start.1 = ((bf16[32,8,576]{2,1,0:T(8,128)(2,1)}), bf16[32,8,576]{2,1,0:T(8,128)(2,1)}, u32[]{:S(2)}, u32[]{:S(2)}) async-start(bf16[32,8,576]{2,1,0:T(8,128)(2,1)} %reshape.135), calls=%async_computation.1 | async-start | bytes 655360 | tf_op jit(solution)/shard_map/all_to_all | solution.py:78
  111.6 0.6 iota_compare_fusion
  112.2 254.0 %all-reduce.2.cloned.1.call-done = bf16[256,1152]{1,0:T(8,128)(2,1)} async-done(((bf16[256,1152]{1,0:T(8,128)(2,1)}), bf16[256,1152]{1,0:T(8,128)(2,1)}) %all-reduce.2.cloned.1.call-update) | async-done | bytes 589840 | tf_op jit(solution)/shard_map/psum | solution.py:13
  366.1 1.4 fusion.14
  367.5 44.5 %all-gather.2 = bf16[32,36,256]{2,1,0:T(8,128)(2,1)S(1)} all-gather(bf16[1,36,256]{2,1,0:T(8,128)(2,1)S(1)} %fusion.14), channel_id=1, replica_groups=mesh['clip'=16,'seq'=32] {'seq'}, dimensions={0}, use_global_device_ids=true | all-gather | bytes 608256 | tf_op jit(solution)/shard_map/all_gather | solution.py:86
  411.9 0.1 reshape.154
  412.1 0.8 fusion.34
  412.8 0.7 copy-done.2
  413.6 0.1 fusion.17
  413.7 21.1 %all-gather.12.cloned.1.call-done = bf16[32,36,576]{2,1,0:T(8,128)(2,1)} async-done(((bf16[1,36,576]{2,1,0:T(8,128)(2,1)}), bf16[32,36,576]{2,1,0:T(8,128)(2,1)}) %all-gather.12.cloned.1.call-update) | async-done | bytes 1327120 | tf_op jit(solution)/shard_map/all_gather | solution.py:73
  434.8 3.5 reshape.152
  438.3 62.6 %all-gather.14.cloned.1.call-done = bf16[32,18,1152]{2,1,0:T(8,128)(2,1)} async-done(((bf16[1,18,1152]{2,1,0:T(8,128)(2,1)}), bf16[32,18,1152]{2,1,0:T(8,128)(2,1)}) %all-gather.14.cloned.1.call-update) | async-done | bytes 1327120 | tf_op jit(solution)/shard_map/all_gather | solution.py:74
  500.9 2.4 reshape.156
  503.3 63.6 %all-gather.16.cloned.1.call-done = bf16[32,36,576]{2,1,0:T(8,128)(2,1)} async-done(((bf16[1,36,576]{2,1,0:T(8,128)(2,1)}), bf16[32,36,576]{2,1,0:T(8,128)(2,1)}) %all-gather.16.cloned.1.call-update) | async-done | bytes 1327120 | tf_op jit(solution)/shard_map/all_gather | solution.py:75
  567.0 2.5 reshape.158
  569.5 0.0 all-to-all-done.1
  569.5 2.2 fusion.2
  571.7 0.6 fusion.36
  572.3 0.1 multiply_reduce_fusion.2
  572.4 0.3 copy-done.3
  572.6 0.6 bitcast_reduce_fusion
  573.2 0.4 copy-done.5
  573.6 0.5 fusion.9
  574.1 1.5 fusion.3
  (17 shorter events, 0.1 us)
Async XLA Ops:
  6.5 359.6 %copy-start = (bf16[1152,36]{0,1:T(8,128)(2,1)S(1)}, bf16[1152,36]{0,1:T(8,128)(2,1)}, u32[]{:S(2)}) copy-start(bf16[1152,36]{0,1:T(8,128)(2,1)} %param.15) | copy-start | bytes 248836
  6.5 3.6 copy-start.6
  6.5 3.7 copy-start.1
  6.5 80.8 %all-gather.10.cloned.1.call-start = ((), (), s32[]{:S(2)}) async-start(), calls=%async_computation.3 | async-start | bytes 4257792 | tf_op jit(solution)/shard_map/all_gather | solution.py:68
  7.3 358.8 %all-reduce.2.cloned.1.call-start = ((), (), s32[]{:S(2)}) async-start(), calls=%async_computation.2 | async-start | bytes 1179648 | tf_op jit(solution)/shard_map/psum | solution.py:13
  8.9 425.9 %all-gather.12.cloned.1.call-start = ((), (), s32[]{:S(2)}) async-start(), calls=%async_computation.4 | async-start | bytes 1689600 | tf_op jit(solution)/shard_map/all_gather | solution.py:73
  9.6 491.3 %all-gather.14.cloned.1.call-start = ((), (), s32[]{:S(2)}) async-start(), calls=%async_computation.5 | async-start | bytes 1824768 | tf_op jit(solution)/shard_map/all_gather | solution.py:74
  16.9 12.1 %copy-start.7 = (s32[32]{0:T(128)S(1)}, s32[32]{0:T(128)}, u32[]{:S(2)}) copy-start(s32[32]{0:T(128)} %param.19) | copy-start | bytes 388
  17.9 31.8 %all-to-all-start = ((bf16[32,2,4608]{2,1,0:T(2,128)(2,1)}), bf16[32,2,4608]{2,1,0:T(2,128)(2,1)S(1)}, u32[]{:S(2)}, u32[]{:S(2)}) async-start(bf16[32,2,4608]{2,1,0:T(2,128)(2,1)} %reshape.164), calls=%async_computation | async-start | bytes 1179648 | tf_op jit(solution)/shard_map/all_to_all | solution.py:64
  28.4 538.6 %all-gather.16.cloned.1.call-start = ((), (), s32[]{:S(2)}) async-start(), calls=%async_computation.6 | async-start | bytes 1689600 | tf_op jit(solution)/shard_map/all_gather | solution.py:75
  99.3 1.9 copy-start.4
  104.9 464.5 %all-to-all-start.1 = ((bf16[32,8,576]{2,1,0:T(8,128)(2,1)}), bf16[32,8,576]{2,1,0:T(8,128)(2,1)}, u32[]{:S(2)}, u32[]{:S(2)}) async-start(bf16[32,8,576]{2,1,0:T(8,128)(2,1)} %reshape.135), calls=%async_computation.1 | async-start | bytes 655360 | tf_op jit(solution)/shard_map/all_to_all | solution.py:78
  412.8 0.8 copy-start.2
  571.7 1.0 copy-start.3
  572.6 1.0 copy-start.5
Sparse Core Ops, SparseCore 0:
  9.5 77.7 all-gather.9
  90.3 275.7 all-reduce.1
  368.5 66.2 all-gather.11
  437.0 63.8 all-gather.13
  503.1 63.7 all-gather.15
where the time goes:
time: 583 us; the launch traced here: 582 us
  waiting for transfers between devices  461 us (79%)
  blocking collectives  44.5 us (8%)
  local copies, waits for them, and re-layouts  23.2 us (4%)
  starting transfers between devices  17.4 us (3%)
  between operations  14.1 us (2%)
  matrix products  11.8 us (2%)
  other arithmetic  10.3 us (2%)
    psum x1, waiting for transfers between devices, spread_2(): return lax.psum(block, axis)  254 us
    all_gather x1, waiting for transfers between devices, per_device(): lax.all_gather(cross_out, 'seq', axis=1, tiled=True)  63.6 us
    all_gather x1, waiting for transfers between devices, per_device(): lax.all_gather(cross_query, 'seq', axis=1, tiled=True)  62.6 us
    all_gather x1, blocking collectives, per_device(): keyval = lax.all_gather(own_columns, 'seq', axis=1, tiled=True)  44.5 us
    all_gather x1, waiting for transfers between devices, per_device(): lax.all_gather(self_proj, 'seq', axis=1, tiled=True)  37.1 us
    all_gather x1, waiting for transfers between devices, per_device(): lax.all_gather(self_out, 'seq', axis=1, tiled=True)  21.1 us
    all_to_all x1, waiting for transfers between devices, per_device(): lax.all_to_all(normed, 'seq', split_axis=1, concat_axis=0, tiled=True)  20.2 us
    unnamed x24, local copies, waits for them, and re-layouts  17.1 us
  transfers between devices with their start and end apart: 7, of which 6 were waited for; matrix products, arithmetic and copies ran while one was open for 7% of the time, Pallas kernels for 0%

commit v1 on v0

--- a/solution.py
+++ b/solution.py
@@ -3,14 +3,16 @@
 import jax.numpy as jnp
 from jax import lax
 from jax.sharding import PartitionSpec as P
+from jax.lax import all_gather
 
 HEAD_DIM = 72
 EPS = 1e-06
+_deliver_numbers = lambda xs, comm_axis: jnp.sum(all_gather(xs, comm_axis), axis=0)
 
 
 def spread_2(block, axis, owner):
     block = jnp.where(lax.axis_index(axis) == owner, block, jnp.zeros_like(block))
-    return lax.psum(block, axis)
+    return _deliver_numbers(block, axis)
 
 
 def layer_norm(values):

time: 583 us -> 471 us (0.81)
  waiting for transfers between devices: 461 us -> 324 us
  blocking collectives: 44.5 us -> 75.9 us
  starting transfers between devices: 17.4 us -> 5.75 us
  other arithmetic: 10.3 us -> 19.1 us
    psum x1 -> x0, waiting for transfers between devices: 254 us -> none  [spread_2(): return lax.psum(block, axis)]
    all_gather x0 -> x1, waiting for transfers between devices: none -> 111 us  [all_gather(xs, comm_axis)]
    all_to_all x0 -> x1, blocking collectives: none -> 30.7 us  [per_device(): lax.all_to_all(normed, 'seq', split_axis=1, concat_axis=0, tiled=True)]
    all_gather x1, waiting for transfers between devices: 21.1 us -> 45.4 us  [per_device(): lax.all_gather(self_out, 'seq', axis=1, tiled=True)]
    all_to_all x1 -> x0, waiting for transfers between devices: 20.2 us -> none  [per_device(): lax.all_to_all(normed, 'seq', split_axis=1, concat_axis=0, tiled=True)]
    all_to_all x1 -> x0, starting transfers between devices: 10.4 us -> none  [per_device(): lax.all_to_all(normed, 'seq', split_axis=1, concat_axis=0, tiled=True)]
    reduce_sum x0 -> x1, other arithmetic: none -> 9.95 us  [jnp.sum(all_gather(xs, comm_axis), axis=0)]
    unnamed x24 -> x22, local copies, waits for them, and re-layouts: 17.1 us -> 15.8 us
  transfers between devices with their start and end apart: 7 -> 6, of which waited for: 6 -> 5; matrix products, arithmetic and copies ran while one was open for 7% -> 8% of each run, Pallas kernels for 0% -> 0%
where the time goes in v1:
time: 471 us; the launch traced here: 470 us
  waiting for transfers between devices  324 us (69%)
  blocking collectives  75.9 us (16%)
  local copies, waits for them, and re-layouts  21 us (4%)
  other arithmetic  19.1 us (4%)
  between operations  14.1 us (3%)
  matrix products  10.7 us (2%)
  starting transfers between devices  5.75 us (1%)
    all_gather x1, waiting for transfers between devices, all_gather(xs, comm_axis)  111 us
    all_gather x1, waiting for transfers between devices, per_device(): lax.all_gather(cross_out, 'seq', axis=1, tiled=True)  63.4 us
    all_gather x1, waiting for transfers between devices, per_device(): lax.all_gather(cross_query, 'seq', axis=1, tiled=True)  63 us
    all_gather x1, waiting for transfers between devices, per_device(): lax.all_gather(self_out, 'seq', axis=1, tiled=True)  45.4 us
    all_gather x1, blocking collectives, per_device(): keyval = lax.all_gather(own_columns, 'seq', axis=1, tiled=True)  45.2 us
    all_gather x1, waiting for transfers between devices, per_device(): lax.all_gather(self_proj, 'seq', axis=1, tiled=True)  38.3 us
    all_to_all x1, blocking collectives, per_device(): lax.all_to_all(normed, 'seq', split_axis=1, concat_axis=0, tiled=True)  30.7 us
    unnamed x22, local copies, waits for them, and re-layouts  15.8 us
  transfers between devices with their start and end apart: 6, of which 5 were waited for; matrix products, arithmetic and copies ran while one was open for 8% of the time, Pallas kernels for 0%

profile of v1, /device:TPU:1, one launch (start us, length us, event | category | flops | bytes accessed | tf_op | source)
XLA Modules:
  0.0 470.1 jit_solution(7402782862727938438)
XLA Ops:
  6.5 0.0 copy-start
  6.5 0.0 all-gather.13.cloned.1.call-start
  6.5 0.7 all-gather.13.cloned.1.call-update
  7.3 0.0 all-gather.15.cloned.1.call-start
  7.3 0.7 all-gather.15.cloned.1.call-update
  8.0 0.0 all-gather.17.cloned.1.call-start
  8.1 0.7 all-gather.17.cloned.1.call-update
  8.7 0.0 all-gather.19.cloned.1.call-start
  8.8 0.5 all-gather.19.cloned.1.call-update
  9.3 0.0 all-gather.11.cloned.1.call-start
  10.0 0.9 broadcast_select_fusion
  10.9 0.0 all-gather.11.cloned.1.call-update
  10.9 0.0 copy-done.5
  11.0 0.0 copy-done.1
  11.0 0.2 convert_reduce_fusion
  11.2 0.3 fusion.10
  11.5 0.3 fusion.13
  11.8 0.9 copy.54
  12.7 0.6 broadcast.111
  13.3 4.4 reduce.9
  17.7 0.2 reshape.161
  17.9 30.7 %all_to_all.8 = bf16[32,2,4608]{2,1,0:T(2,128)(2,1)S(1)} all-to-all(bf16[32,2,4608]{2,1,0:T(2,128)(2,1)S(1)} %reshape.161), channel_id=1, replica_groups=mesh['clip'=16,'seq'=32] {'seq'}, dimensions={0} | all-to-all | bytes 1179648 | tf_op jit(solution)/shard_map/all_to_all | solution.py:66
  48.6 0.5 reshape.162
  49.1 38.3 %all-gather.13.cloned.1.call-done = bf16[32,54,1152]{2,1,0:T(8,128)(2,1)} async-done(((bf16[1,54,1152]{2,1,0:T(8,128)(2,1)}), bf16[32,54,1152]{2,1,0:T(8,128)(2,1)}) %all-gather.13.cloned.1.call-update) | async-done | bytes 3981328 | tf_op jit(solution)/shard_map/all_gather | solution.py:70
  87.4 5.1 %reshape.147 = bf16[1728,1152]{1,0:T(8,128)(2,1)} reshape(bf16[32,54,1152]{2,1,0:T(8,128)(2,1)} %all-gather.13.cloned.1.call-done) | data formatting | bytes 7962624
  92.4 3.5 convolution_convert_fusion
  95.9 0.6 copy.29
  96.5 0.2 slice_convert_fusion.1
  96.7 1.3 reshape.127
  98.1 0.5 reshape.143
  98.6 0.5 reshape.141
  99.0 0.3 multiply_reduce_fusion
  99.4 0.3 multiply_reduce_fusion.1
  99.8 0.7 multiply_convert_fusion
  100.5 0.9 fusion.35
  101.5 0.1 copy-done.4
  101.6 0.7 fusion.7
  102.3 0.0 copy-start.6
  102.3 0.2 copy.34
  102.5 1.1 reshape.132
  103.6 5.6 %all-to-all-start.1 = ((bf16[32,8,576]{2,1,0:T(8,128)(2,1)}), bf16[32,8,576]{2,1,0:T(8,128)(2,1)}, u32[]{:S(2)}, u32[]{:S(2)}) async-start(bf16[32,8,576]{2,1,0:T(8,128)(2,1)} %reshape.132), calls=%async_computation.1 | async-start | bytes 655360 | tf_op jit(solution)/shard_map/all_to_all | solution.py:80
  109.2 0.7 fusion.31
  109.9 0.6 iota_compare_fusion
  110.5 45.4 %all-gather.15.cloned.1.call-done = bf16[32,36,576]{2,1,0:T(8,128)(2,1)} async-done(((bf16[1,36,576]{2,1,0:T(8,128)(2,1)}), bf16[32,36,576]{2,1,0:T(8,128)(2,1)}) %all-gather.15.cloned.1.call-update) | async-done | bytes 1327120 | tf_op jit(solution)/shard_map/all_gather | solution.py:75
  155.9 3.5 reshape.149
  159.4 63.0 %all-gather.17.cloned.1.call-done = bf16[32,18,1152]{2,1,0:T(8,128)(2,1)} async-done(((bf16[1,18,1152]{2,1,0:T(8,128)(2,1)}), bf16[32,18,1152]{2,1,0:T(8,128)(2,1)}) %all-gather.17.cloned.1.call-update) | async-done | bytes 1327120 | tf_op jit(solution)/shard_map/all_gather | solution.py:76
  222.4 2.4 reshape.153
  224.8 63.4 %all-gather.19.cloned.1.call-done = bf16[32,36,576]{2,1,0:T(8,128)(2,1)} async-done(((bf16[1,36,576]{2,1,0:T(8,128)(2,1)}), bf16[32,36,576]{2,1,0:T(8,128)(2,1)}) %all-gather.19.cloned.1.call-update) | async-done | bytes 1327120 | tf_op jit(solution)/shard_map/all_gather | solution.py:77
  288.3 2.5 reshape.155
  290.8 0.0 all-to-all-done.1
  290.8 2.2 fusion.2
  293.0 0.6 fusion.36
  293.6 0.1 multiply_reduce_fusion.2
  293.7 0.2 copy-done.2
  293.8 110.9 %all-gather.11.cloned.1.call-done = bf16[32,256,1152]{2,1,0:T(8,128)(2,1)} async-done(((bf16[1,256,1152]{2,1,0:T(8,128)(2,1)}), bf16[32,256,1152]{2,1,0:T(8,128)(2,1)}) %all-gather.11.cloned.1.call-update) | async-done | bytes 18874384 | tf_op jit(solution)/shard_map/all_gather | solution.py:10
  404.7 10.0 %reduce_sum.98 = bf16[256,1152]{1,0:T(8,128)(2,1)S(1)} reduce(bf16[32,256,1152]{2,1,0:T(8,128)(2,1)} %all-gather.11.cloned.1.call-done, bf16[]{:T(256)} %constant.29.clone.1), dimensions={0}, to_apply=%region_5.6 | reduce | flops 9142272 | bytes 19464194 | tf_op jit(solution)/shard_map/reduce_sum | solution.py:10
  414.7 0.3 fusion.14
  415.0 45.2 %all-gather.2 = bf16[32,36,256]{2,1,0:T(8,128)(2,1)S(1)} all-gather(bf16[1,36,256]{2,1,0:T(8,128)(2,1)S(1)} %fusion.14), channel_id=1, replica_groups=mesh['clip'=16,'seq'=32] {'seq'}, dimensions={0}, use_global_device_ids=true | all-gather | bytes 608256 | tf_op jit(solution)/shard_map/all_gather | solution.py:88
  460.2 0.1 reshape.151
  460.3 0.1 fusion.17
  460.4 0.6 bitcast_reduce_fusion
  461.0 0.5 fusion.9
  461.5 0.6 copy-done.3
  462.1 1.5 fusion.3
  (15 shorter events, 0.2 us)
Async XLA Ops:
  6.5 408.1 %copy-start = (bf16[1152,36]{0,1:T(8,128)(2,1)S(1)}, bf16[1152,36]{0,1:T(8,128)(2,1)}, u32[]{:S(2)}) copy-start(bf16[1152,36]{0,1:T(8,128)(2,1)} %param.15) | copy-start | bytes 248836
  6.5 4.4 copy-start.5
  6.5 4.4 copy-start.1
  6.5 80.8 %all-gather.13.cloned.1.call-start = ((), (), s32[]{:S(2)}) async-start(), calls=%async_computation.3 | async-start | bytes 4257792 | tf_op jit(solution)/shard_map/all_gather | solution.py:70
  7.3 148.6 %all-gather.15.cloned.1.call-start = ((), (), s32[]{:S(2)}) async-start(), calls=%async_computation.4 | async-start | bytes 1689600 | tf_op jit(solution)/shard_map/all_gather | solution.py:75
  8.0 214.4 %all-gather.17.cloned.1.call-start = ((), (), s32[]{:S(2)}) async-start(), calls=%async_computation.5 | async-start | bytes 1824768 | tf_op jit(solution)/shard_map/all_gather | solution.py:76
  8.7 279.5 %all-gather.19.cloned.1.call-start = ((), (), s32[]{:S(2)}) async-start(), calls=%async_computation.6 | async-start | bytes 1689600 | tf_op jit(solution)/shard_map/all_gather | solution.py:77
  9.3 395.4 %all-gather.11.cloned.1.call-start = ((), (), s32[]{:S(2)}) async-start(), calls=%async_computation.2 | async-start | bytes 19464192 | tf_op jit(solution)/shard_map/all_gather | solution.py:10
  100.5 1.0 copy-start.4
  102.3 6.9 %copy-start.6 = (s32[32]{0:T(128)S(1)}, s32[32]{0:T(128)}, u32[]{:S(2)}) copy-start(s32[32]{0:T(128)} %param.19) | copy-start | bytes 388
  103.6 187.2 %all-to-all-start.1 = ((bf16[32,8,576]{2,1,0:T(8,128)(2,1)}), bf16[32,8,576]{2,1,0:T(8,128)(2,1)}, u32[]{:S(2)}, u32[]{:S(2)}) async-start(bf16[32,8,576]{2,1,0:T(8,128)(2,1)} %reshape.132), calls=%async_computation.1 | async-start | bytes 655360 | tf_op jit(solution)/shard_map/all_to_all | solution.py:80
  293.0 0.8 copy-start.2
  461.0 1.1 copy-start.3
Sparse Core Ops, SparseCore 0:
  9.5 77.8 all-gather.12
  89.5 66.3 all-gather.14
  158.1 64.3 all-gather.16
  224.4 63.7 all-gather.18
  290.3 114.4 all-gather.10
